TPU v7x, 32 devices: a whole 2x2x4 slice. The times are simulated.
32 devices in a mesh: parts: 2 (over x), rows: 2 (over core), cols: 8 (over z, y).
Axes of the slice: x: 2, y: 2, z: 4, core: 2. Of those that a mesh axis runs over, the one named last changes fastest.
Arguments:
- src_feat: float32 [32, 131072], P(None, ('parts', 'rows', 'cols')), parts along dimension 1, may hold values from -0.75 to 0.75
- tgt_feat: float32 [32, 16384], P(None, ('parts', 'cols')), parts along dimension 1, may hold values from -0.75 to 0.75
- tgt_pot: float32 [16384], P(('parts', 'cols')), parts along dimension 0, may hold values from -25 to 25
- log_src: float32 [131072], P(('parts', 'rows', 'cols')), parts along dimension 0, may hold values from -3 to 3
- log_tgt: float32 [16384], P(('parts', 'cols')), parts along dimension 0, may hold values from -3 to 3
- pairs: int32 [512, 24], P(('parts', 'rows', 'cols')), parts along dimension 0, may hold values from 0 to 31, as said below
- counts: int32 [512], P(('parts', 'rows', 'cols')), parts along dimension 0, may hold values from 1 to 24, as said below
Outputs:
- src_pot: float32 [131072], P(('parts', 'rows', 'cols')), parts along dimension 0
- new_tgt_pot: float32 [16384], P(('parts', 'cols')), parts along dimension 0
There are 2 independent parts, one for each index of `parts`. A program takes and returns all parts, laid end to end along the dimension named above; each array names one. Nothing has to cross between parts.
Inputs may be any that keep to these rules, and one draw needn't show every extreme that they name: `pairs`: each row names 24 different target blocks, and every target block is the first entry of some row. `counts`: row 0 uses all 24 entries and row 1 only one.
All inputs are finite; a program needn't handle non-finite values.
Results may differ from a plain program's by a relative error of at most 0.0003.
Values sent between devices are 32-bit elements; how exact they have to be, the bound alone decides.
No kernel may reach another device: no remote copies, remote signals or barrier semaphores. Data moves between devices by JAX's collectives and lax.ppermute only.
A program may use at most 128 MiB of HBM per device.

v0:
```python
import jax
import jax.numpy as jnp
from jax import lax
from jax.sharding import PartitionSpec as P

D = 32
BLK = 256
GROUP = 8
epsilon = 0.1
NEG = -1e30


def joined(array, axis, combine):
    everything = jax.tree.map(lambda part: lax.all_gather(part, axis), array)
    initial = jax.tree.map(lambda part: part[0], everything)

    def step(k, so_far):
        return combine(so_far, jax.tree.map(lambda part: part[k], everything))

    return lax.fori_loop(1, lax.axis_size(axis), step, initial)


def combine_parts(first, second):
    top = jnp.maximum(first[0], second[0])
    total = first[1] * jnp.exp(first[0] - top) + second[1] * jnp.exp(second[0] - top)
    return (top, total)


def on_device(src_feat, tgt_feat, tgt_pot, log_src, log_tgt, pairs, counts):
    own_targets = tgt_feat.shape[1]
    packed = jnp.concatenate([tgt_feat, tgt_pot[None, :], log_tgt[None, :]], axis=0)
    whole = lax.all_gather(packed, "cols", axis=1, tiled=True)
    feats = whole[:D]
    ynorm = jnp.sum(feats * feats, axis=0)
    tblocks = whole.shape[1] // BLK
    table = jnp.concatenate([whole, ynorm[None, :]], axis=0)
    blocks = jnp.transpose(table.reshape(D + 3, tblocks, BLK), (1, 0, 2))
    within = jnp.arange(GROUP, dtype=jnp.int32)
    block_numbers = jnp.arange(tblocks, dtype=jnp.int32)

    def row_step(carry, index):
        start = index * BLK
        xs = lax.dynamic_slice_in_dim(src_feat, start, BLK, 1)
        weights = lax.dynamic_slice_in_dim(log_src, start, BLK, 0)
        xnorm = jnp.sum(xs * xs, axis=0)
        row_ids = pairs[index]
        count = counts[index]
        ngroups = (count + GROUP - 1) // GROUP
        slabs = jnp.take(blocks, row_ids, axis=0)

        def take_group(step):
            ids = lax.dynamic_slice_in_dim(row_ids, step * GROUP, GROUP, 0)
            group = lax.dynamic_slice_in_dim(slabs, step * GROUP, GROUP, 0)
            mask = jnp.repeat(step * GROUP + within < count, BLK)
            cross = jnp.einsum(
                "dr,gdc->rgc",
                xs,
                group[:, :D, :],
                precision=lax.Precision.HIGHEST,
                preferred_element_type=jnp.float32,
            ).reshape(BLK, GROUP * BLK)
            cost = xnorm[:, None] + group[:, D + 2, :].reshape(-1)[None, :] - 2.0 * cross
            return (ids, mask, group, cost)

        def row_pass(step, state):
            run_top, run_sum = state
            ids, mask, group, cost = take_group(step)
            pots = group[:, D, :].reshape(-1)
            logs = group[:, D + 1, :].reshape(-1)
            scores = jnp.where(mask[None, :], logs[None, :] + (pots[None, :] - cost) / epsilon, NEG)
            top = jnp.maximum(run_top, jnp.max(scores, axis=1))
            run_sum = run_sum * jnp.exp(run_top - top) + jnp.sum(
                jnp.exp(scores - top[:, None]), axis=1
            )
            return (top, run_sum)

        start_state = (jnp.full((BLK,), NEG, jnp.float32), jnp.zeros((BLK,), jnp.float32))
        run_top, run_sum = lax.fori_loop(0, ngroups, row_pass, start_state)
        fpot = -epsilon * (run_top + jnp.log(run_sum))

        def col_pass(step, state):
            acc_top, acc_sum = state
            ids, mask, group, cost = take_group(step)
            scores = jnp.where(
                mask[None, :], weights[:, None] + (fpot[:, None] - cost) / epsilon, NEG
            )
            col_top = jnp.max(scores, axis=0)
            col_sum = jnp.where(mask, jnp.sum(jnp.exp(scores - col_top[None, :]), axis=0), 0.0)
            col_top = col_top.reshape(GROUP, BLK)
            col_sum = col_sum.reshape(GROUP, BLK)
            selector = ids[:, None] == block_numbers[None, :]
            onehot = selector.astype(jnp.float32)
            landed = jnp.max(jnp.where(selector[:, :, None], col_top[:, None, :], NEG), axis=0)
            top = jnp.maximum(acc_top, landed)
            top_here = jnp.einsum(
                "gt,tb->gb",
                onehot,
                top,
                precision=lax.Precision.HIGHEST,
                preferred_element_type=jnp.float32,
            )
            added = jnp.einsum(
                "gt,gb->tb",
                onehot,
                col_sum * jnp.exp(col_top - top_here),
                precision=lax.Precision.HIGHEST,
                preferred_element_type=jnp.float32,
            )
            fresh = acc_sum * jnp.exp(acc_top - top) + added
            return (top, fresh)

        carry = lax.fori_loop(0, ngroups, col_pass, carry)
        return (carry, fpot)

    init = (jnp.full((tblocks, BLK), NEG, jnp.float32), jnp.zeros((tblocks, BLK), jnp.float32))
    (acc_top, acc_sum), fblocks = lax.scan(
        row_step, init, jnp.arange(pairs.shape[0], dtype=jnp.int32)
    )
    src_pot = fblocks.reshape(-1)
    flat_top = acc_top.reshape(-1)
    flat_sum = acc_sum.reshape(-1)
    owner_start = lax.axis_index("cols") * own_targets
    all_top, all_sum = joined((flat_top, flat_sum), ("rows", "cols"), combine_parts)
    own_top = lax.dynamic_slice_in_dim(all_top, owner_start, own_targets, 0)
    own_sum = lax.dynamic_slice_in_dim(all_sum, owner_start, own_targets, 0)
    new_tgt_pot = -epsilon * (own_top + jnp.log(own_sum))
    return (src_pot, new_tgt_pot)


def solution(mesh):
    placed = (
        P(None, ("parts", "rows", "cols")),
        P(None, ("parts", "cols")),
        P(("parts", "cols")),
        P(("parts", "rows", "cols")),
        P(("parts", "cols")),
        P(("parts", "rows", "cols"), None),
        P(("parts", "rows", "cols")),
    )
    return jax.shard_map(
        on_device,
        mesh=mesh,
        in_specs=placed,
        out_specs=(P(("parts", "rows", "cols")), P(("parts", "cols"))),
        check_vma=False,
    )
```

profile of v0, /device:TPU:0, one launch (start us, length us, event | category | flops | bytes accessed | tf_op | source)
XLA Modules:
  0.0 660.8 jit_solution(5542897578245292571)
XLA Ops:
  8.9 46.1 %all-gather.4.cloned.1.call-done = f32[34,8192]{1,0:T(8,128)} async-done(((f32[34,1024]{1,0:T(8,128)}), f32[34,8192]{1,0:T(8,128)}) %all-gather.4.cloned.1.call-update) | async-done | bytes 1114128 | tf_op jit(solution)/shard_map/all_gather | solution.py:32
  57.9 446.4 %while.113 = (s32[]{:T(128)}, f32[32,256]{1,0:T(8,128)S(1)}, f32[32,256]{1,0:T(8,128)S(1)}, f32[16,256]{1,0:T(8,128)S(1)}, s32[16]{0:T(128)S(1)}, /*index=5*/s32...) while((s32[]{:T(128)}, f32[32,256]{1,0:T(8,128)S(1)}, ...), condition=%wide.region_12.13_spmd.clone.clone, body=%wide.region_1.12_spmd.clone.clone.sunk | while | flops 415103776 | bytes 13110493 | solution.py:116
  65.5 12.1 %while.114 = (s32[]{:T(128)}, f32[256]{0:T(256)S(1)}, f32[256]{0:T(256)S(1)}, s32[]{:T(128)}, s32[8]{0:T(128)S(1)}, /*index=5*/s32[]{:T(128)}, f32[24,35,256]{2,...) while((s32[]{:T(128)}, f32[256]{0:T(256)S(1)}, ...), condition=%wide.region_6.6_spmd, body=%wide.region_3.5_spmd.sunk | while | flops 206570016 | bytes 4627243 | solution.py:78
  78.4 12.5 %while.115 = (s32[]{:T(128)}, f32[32,256]{1,0:T(8,128)S(1)}, f32[32,256]{1,0:T(8,128)S(1)}, s32[]{:T(128)}, s32[24]{0:T(128)S(1)}, /*index=5*/s32[32]{0:T(128)S(...) while((s32[]{:T(128)}, f32[32,256]{1,0:T(8,128)S(1)}, ...), condition=%wide.region_11.11_spmd, body=%wide.region_7.10_spmd.sunk | while | flops 208300816 | bytes 4961095 | solution.py:112
  115.1 12.1 %while.114 = (s32[]{:T(128)}, f32[256]{0:T(256)S(1)}, f32[256]{0:T(256)S(1)}, s32[]{:T(128)}, s32[8]{0:T(128)S(1)}, /*index=5*/s32[]{:T(128)}, f32[24,35,256]{2,...) while((s32[]{:T(128)}, f32[256]{0:T(256)S(1)}, ...), condition=%wide.region_6.6_spmd, body=%wide.region_3.5_spmd.sunk | while | flops 206570016 | bytes 4627243 | solution.py:78
  128.0 12.5 %while.115 = (s32[]{:T(128)}, f32[32,256]{1,0:T(8,128)S(1)}, f32[32,256]{1,0:T(8,128)S(1)}, s32[]{:T(128)}, s32[24]{0:T(128)S(1)}, /*index=5*/s32[32]{0:T(128)S(...) while((s32[]{:T(128)}, f32[32,256]{1,0:T(8,128)S(1)}, ...), condition=%wide.region_11.11_spmd, body=%wide.region_7.10_spmd.sunk | while | flops 208300816 | bytes 4961095 | solution.py:112
  148.1 8.1 %while.114 = (s32[]{:T(128)}, f32[256]{0:T(256)S(1)}, f32[256]{0:T(256)S(1)}, s32[]{:T(128)}, s32[8]{0:T(128)S(1)}, /*index=5*/s32[]{:T(128)}, f32[24,35,256]{2,...) while((s32[]{:T(128)}, f32[256]{0:T(256)S(1)}, ...), condition=%wide.region_6.6_spmd, body=%wide.region_3.5_spmd.sunk | while | flops 206570016 | bytes 4627243 | solution.py:78
  157.0 8.3 %while.115 = (s32[]{:T(128)}, f32[32,256]{1,0:T(8,128)S(1)}, f32[32,256]{1,0:T(8,128)S(1)}, s32[]{:T(128)}, s32[24]{0:T(128)S(1)}, /*index=5*/s32[32]{0:T(128)S(...) while((s32[]{:T(128)}, f32[32,256]{1,0:T(8,128)S(1)}, ...), condition=%wide.region_11.11_spmd, body=%wide.region_7.10_spmd.sunk | while | flops 208300816 | bytes 4961095 | solution.py:112
  173.0 12.1 %while.114 = (s32[]{:T(128)}, f32[256]{0:T(256)S(1)}, f32[256]{0:T(256)S(1)}, s32[]{:T(128)}, s32[8]{0:T(128)S(1)}, /*index=5*/s32[]{:T(128)}, f32[24,35,256]{2,...) while((s32[]{:T(128)}, f32[256]{0:T(256)S(1)}, ...), condition=%wide.region_6.6_spmd, body=%wide.region_3.5_spmd.sunk | while | flops 206570016 | bytes 4627243 | solution.py:78
  185.9 12.5 %while.115 = (s32[]{:T(128)}, f32[32,256]{1,0:T(8,128)S(1)}, f32[32,256]{1,0:T(8,128)S(1)}, s32[]{:T(128)}, s32[24]{0:T(128)S(1)}, /*index=5*/s32[32]{0:T(128)S(...) while((s32[]{:T(128)}, f32[32,256]{1,0:T(8,128)S(1)}, ...), condition=%wide.region_11.11_spmd, body=%wide.region_7.10_spmd.sunk | while | flops 208300816 | bytes 4961095 | solution.py:112
  206.0 12.1 %while.114 = (s32[]{:T(128)}, f32[256]{0:T(256)S(1)}, f32[256]{0:T(256)S(1)}, s32[]{:T(128)}, s32[8]{0:T(128)S(1)}, /*index=5*/s32[]{:T(128)}, f32[24,35,256]{2,...) while((s32[]{:T(128)}, f32[256]{0:T(256)S(1)}, ...), condition=%wide.region_6.6_spmd, body=%wide.region_3.5_spmd.sunk | while | flops 206570016 | bytes 4627243 | solution.py:78
  218.9 12.5 %while.115 = (s32[]{:T(128)}, f32[32,256]{1,0:T(8,128)S(1)}, f32[32,256]{1,0:T(8,128)S(1)}, s32[]{:T(128)}, s32[24]{0:T(128)S(1)}, /*index=5*/s32[32]{0:T(128)S(...) while((s32[]{:T(128)}, f32[32,256]{1,0:T(8,128)S(1)}, ...), condition=%wide.region_11.11_spmd, body=%wide.region_7.10_spmd.sunk | while | flops 208300816 | bytes 4961095 | solution.py:112
  247.9 8.3 %while.115 = (s32[]{:T(128)}, f32[32,256]{1,0:T(8,128)S(1)}, f32[32,256]{1,0:T(8,128)S(1)}, s32[]{:T(128)}, s32[24]{0:T(128)S(1)}, /*index=5*/s32[32]{0:T(128)S(...) while((s32[]{:T(128)}, f32[32,256]{1,0:T(8,128)S(1)}, ...), condition=%wide.region_11.11_spmd, body=%wide.region_7.10_spmd.sunk | while | flops 208300816 | bytes 4961095 | solution.py:112
  263.8 12.1 %while.114 = (s32[]{:T(128)}, f32[256]{0:T(256)S(1)}, f32[256]{0:T(256)S(1)}, s32[]{:T(128)}, s32[8]{0:T(128)S(1)}, /*index=5*/s32[]{:T(128)}, f32[24,35,256]{2,...) while((s32[]{:T(128)}, f32[256]{0:T(256)S(1)}, ...), condition=%wide.region_6.6_spmd, body=%wide.region_3.5_spmd.sunk | while | flops 206570016 | bytes 4627243 | solution.py:78
  276.8 12.5 %while.115 = (s32[]{:T(128)}, f32[32,256]{1,0:T(8,128)S(1)}, f32[32,256]{1,0:T(8,128)S(1)}, s32[]{:T(128)}, s32[24]{0:T(128)S(1)}, /*index=5*/s32[32]{0:T(128)S(...) while((s32[]{:T(128)}, f32[32,256]{1,0:T(8,128)S(1)}, ...), condition=%wide.region_11.11_spmd, body=%wide.region_7.10_spmd.sunk | while | flops 208300816 | bytes 4961095 | solution.py:112
  296.9 8.1 %while.114 = (s32[]{:T(128)}, f32[256]{0:T(256)S(1)}, f32[256]{0:T(256)S(1)}, s32[]{:T(128)}, s32[8]{0:T(128)S(1)}, /*index=5*/s32[]{:T(128)}, f32[24,35,256]{2,...) while((s32[]{:T(128)}, f32[256]{0:T(256)S(1)}, ...), condition=%wide.region_6.6_spmd, body=%wide.region_3.5_spmd.sunk | while | flops 206570016 | bytes 4627243 | solution.py:78
  305.8 8.3 %while.115 = (s32[]{:T(128)}, f32[32,256]{1,0:T(8,128)S(1)}, f32[32,256]{1,0:T(8,128)S(1)}, s32[]{:T(128)}, s32[24]{0:T(128)S(1)}, /*index=5*/s32[32]{0:T(128)S(...) while((s32[]{:T(128)}, f32[32,256]{1,0:T(8,128)S(1)}, ...), condition=%wide.region_11.11_spmd, body=%wide.region_7.10_spmd.sunk | while | flops 208300816 | bytes 4961095 | solution.py:112
  321.7 8.1 %while.114 = (s32[]{:T(128)}, f32[256]{0:T(256)S(1)}, f32[256]{0:T(256)S(1)}, s32[]{:T(128)}, s32[8]{0:T(128)S(1)}, /*index=5*/s32[]{:T(128)}, f32[24,35,256]{2,...) while((s32[]{:T(128)}, f32[256]{0:T(256)S(1)}, ...), condition=%wide.region_6.6_spmd, body=%wide.region_3.5_spmd.sunk | while | flops 206570016 | bytes 4627243 | solution.py:78
  330.6 8.3 %while.115 = (s32[]{:T(128)}, f32[32,256]{1,0:T(8,128)S(1)}, f32[32,256]{1,0:T(8,128)S(1)}, s32[]{:T(128)}, s32[24]{0:T(128)S(1)}, /*index=5*/s32[32]{0:T(128)S(...) while((s32[]{:T(128)}, f32[32,256]{1,0:T(8,128)S(1)}, ...), condition=%wide.region_11.11_spmd, body=%wide.region_7.10_spmd.sunk | while | flops 208300816 | bytes 4961095 | solution.py:112
  346.5 8.1 %while.114 = (s32[]{:T(128)}, f32[256]{0:T(256)S(1)}, f32[256]{0:T(256)S(1)}, s32[]{:T(128)}, s32[8]{0:T(128)S(1)}, /*index=5*/s32[]{:T(128)}, f32[24,35,256]{2,...) while((s32[]{:T(128)}, f32[256]{0:T(256)S(1)}, ...), condition=%wide.region_6.6_spmd, body=%wide.region_3.5_spmd.sunk | while | flops 206570016 | bytes 4627243 | solution.py:78
  355.4 8.3 %while.115 = (s32[]{:T(128)}, f32[32,256]{1,0:T(8,128)S(1)}, f32[32,256]{1,0:T(8,128)S(1)}, s32[]{:T(128)}, s32[24]{0:T(128)S(1)}, /*index=5*/s32[32]{0:T(128)S(...) while((s32[]{:T(128)}, f32[32,256]{1,0:T(8,128)S(1)}, ...), condition=%wide.region_11.11_spmd, body=%wide.region_7.10_spmd.sunk | while | flops 208300816 | bytes 4961095 | solution.py:112
  371.3 8.1 %while.114 = (s32[]{:T(128)}, f32[256]{0:T(256)S(1)}, f32[256]{0:T(256)S(1)}, s32[]{:T(128)}, s32[8]{0:T(128)S(1)}, /*index=5*/s32[]{:T(128)}, f32[24,35,256]{2,...) while((s32[]{:T(128)}, f32[256]{0:T(256)S(1)}, ...), condition=%wide.region_6.6_spmd, body=%wide.region_3.5_spmd.sunk | while | flops 206570016 | bytes 4627243 | solution.py:78
  380.2 8.3 %while.115 = (s32[]{:T(128)}, f32[32,256]{1,0:T(8,128)S(1)}, f32[32,256]{1,0:T(8,128)S(1)}, s32[]{:T(128)}, s32[24]{0:T(128)S(1)}, /*index=5*/s32[32]{0:T(128)S(...) while((s32[]{:T(128)}, f32[32,256]{1,0:T(8,128)S(1)}, ...), condition=%wide.region_11.11_spmd, body=%wide.region_7.10_spmd.sunk | while | flops 208300816 | bytes 4961095 | solution.py:112
  396.1 8.1 %while.114 = (s32[]{:T(128)}, f32[256]{0:T(256)S(1)}, f32[256]{0:T(256)S(1)}, s32[]{:T(128)}, s32[8]{0:T(128)S(1)}, /*index=5*/s32[]{:T(128)}, f32[24,35,256]{2,...) while((s32[]{:T(128)}, f32[256]{0:T(256)S(1)}, ...), condition=%wide.region_6.6_spmd, body=%wide.region_3.5_spmd.sunk | while | flops 206570016 | bytes 4627243 | solution.py:78
  405.0 8.3 %while.115 = (s32[]{:T(128)}, f32[32,256]{1,0:T(8,128)S(1)}, f32[32,256]{1,0:T(8,128)S(1)}, s32[]{:T(128)}, s32[24]{0:T(128)S(1)}, /*index=5*/s32[32]{0:T(128)S(...) while((s32[]{:T(128)}, f32[32,256]{1,0:T(8,128)S(1)}, ...), condition=%wide.region_11.11_spmd, body=%wide.region_7.10_spmd.sunk | while | flops 208300816 | bytes 4961095 | solution.py:112
  421.0 12.1 %while.114 = (s32[]{:T(128)}, f32[256]{0:T(256)S(1)}, f32[256]{0:T(256)S(1)}, s32[]{:T(128)}, s32[8]{0:T(128)S(1)}, /*index=5*/s32[]{:T(128)}, f32[24,35,256]{2,...) while((s32[]{:T(128)}, f32[256]{0:T(256)S(1)}, ...), condition=%wide.region_6.6_spmd, body=%wide.region_3.5_spmd.sunk | while | flops 206570016 | bytes 4627243 | solution.py:78
  433.9 12.5 %while.115 = (s32[]{:T(128)}, f32[32,256]{1,0:T(8,128)S(1)}, f32[32,256]{1,0:T(8,128)S(1)}, s32[]{:T(128)}, s32[24]{0:T(128)S(1)}, /*index=5*/s32[32]{0:T(128)S(...) while((s32[]{:T(128)}, f32[32,256]{1,0:T(8,128)S(1)}, ...), condition=%wide.region_11.11_spmd, body=%wide.region_7.10_spmd.sunk | while | flops 208300816 | bytes 4961095 | solution.py:112
  454.0 12.1 %while.114 = (s32[]{:T(128)}, f32[256]{0:T(256)S(1)}, f32[256]{0:T(256)S(1)}, s32[]{:T(128)}, s32[8]{0:T(128)S(1)}, /*index=5*/s32[]{:T(128)}, f32[24,35,256]{2,...) while((s32[]{:T(128)}, f32[256]{0:T(256)S(1)}, ...), condition=%wide.region_6.6_spmd, body=%wide.region_3.5_spmd.sunk | while | flops 206570016 | bytes 4627243 | solution.py:78
  466.9 12.5 %while.115 = (s32[]{:T(128)}, f32[32,256]{1,0:T(8,128)S(1)}, f32[32,256]{1,0:T(8,128)S(1)}, s32[]{:T(128)}, s32[24]{0:T(128)S(1)}, /*index=5*/s32[32]{0:T(128)S(...) while((s32[]{:T(128)}, f32[32,256]{1,0:T(8,128)S(1)}, ...), condition=%wide.region_11.11_spmd, body=%wide.region_7.10_spmd.sunk | while | flops 208300816 | bytes 4961095 | solution.py:112
  495.9 8.3 %while.115 = (s32[]{:T(128)}, f32[32,256]{1,0:T(8,128)S(1)}, f32[32,256]{1,0:T(8,128)S(1)}, s32[]{:T(128)}, s32[24]{0:T(128)S(1)}, /*index=5*/s32[32]{0:T(128)S(...) while((s32[]{:T(128)}, f32[32,256]{1,0:T(8,128)S(1)}, ...), condition=%wide.region_11.11_spmd, body=%wide.region_7.10_spmd.sunk | while | flops 208300816 | bytes 4961095 | solution.py:112
  504.4 114.5 %all-gather.1 = f32[16,1,8192]{2,1,0:T(1,128)S(1)} all-gather(f32[1,1,8192]{2,1,0:T(1,128)S(1)} %reshape.237), channel_id=1, replica_groups=mesh['parts'=2,'rows'=2,'cols'=8] {'rows','cols'}, dimensions={0}, use_global_device_ids=true | all-gather | bytes 557056 | tf_op jit(solution)/shard_map/all_gather | solution.py:14
  619.2 31.4 %all-gather = f32[16,1,8192]{2,1,0:T(1,128)S(1)} all-gather(f32[1,1,8192]{2,1,0:T(1,128)S(1)} %reshape.235), channel_id=1, replica_groups=mesh['parts'=2,'rows'=2,'cols'=8] {'rows','cols'}, dimensions={0}, use_global_device_ids=true | all-gather | bytes 557056 | tf_op jit(solution)/shard_map/all_gather | solution.py:14
  (1098 shorter events, 421.4 us)
Async XLA Ops:
  7.2 47.8 %all-gather.4.cloned.1.call-start = ((), (), s32[]{:S(2)}) async-start(), calls=%async_computation | async-start | bytes 1474560 | tf_op jit(solution)/shard_map/all_gather | solution.py:32
  55.0 2.0 copy-start
  57.1 0.9 copy-start.1
Sparse Core Ops, SparseCore 0:
  10.2 44.7 all-gather.3
where the time goes:
time: 665 us; the launch traced here: 661 us
  matrix products  216 us (32%)
  blocking collectives  146 us (22%)
  other arithmetic  126 us (19%)
  loops' own time  59.5 us (9%)
  local copies, waits for them, and re-layouts  53.3 us (8%)
  waiting for transfers between devices  46.1 us (7%)
  between operations  14.2 us (2%)
    dot_general x76, matrix products, take_group(): jnp.einsum('dr,gdc->rgc', xs, group[:, :D, :], precision=lax.Precision.HI...  198 us
    all_gather x2, blocking collectives, joined(): everything = jax.tree.map(lambda part: lax.all_gather(part, axis), array)  146 us
    another operation x1, loops' own time, on_device(): lax.scan(row_step, init, jnp.arange(pairs.shape[0], dtype=jnp.int32))  53.5 us
    lt x76, other arithmetic, take_group(): mask = jnp.repeat(step * GROUP + within < count, BLK)  52.8 us
    all_gather x1, waiting for transfers between devices, on_device(): whole = lax.all_gather(packed, 'cols', axis=1, tiled=True)  46.1 us
    reduce_sum x38, other arithmetic, row_pass(): jnp.sum(jnp.exp(scores - top[:, None]), axis=1)  13.7 us
    select_n x32, other arithmetic, row_step(): slabs = jnp.take(blocks, row_ids, axis=0)  13.3 us
  transfers between devices with their start and end apart: 1, of which 1 were waited for; matrix products, arithmetic and copies ran while one was open for 0% of the time, Pallas kernels for 0%

commit v1 on v0

--- a/solution.py
+++ b/solution.py
@@ -8,6 +8,17 @@
 GROUP = 8
 epsilon = 0.1
 NEG = -1e30
+
+
+def turned_line(array, axis, d):
+    size = lax.axis_size(axis)
+    right = [(i, (i + 1) % size) for i in range(size)]
+    terms = [array]
+    for stride in range(1, size):
+        terms = [lax.ppermute(terms[0], axis, right), *terms]
+    full = jnp.concatenate(terms, axis=d)
+    shift = (lax.axis_index(axis) + 1) * terms[-1].shape[d]
+    return jnp.roll(full, shift, axis=d)
 
 
 def joined(array, axis, combine):
@@ -29,7 +40,7 @@
 def on_device(src_feat, tgt_feat, tgt_pot, log_src, log_tgt, pairs, counts):
     own_targets = tgt_feat.shape[1]
     packed = jnp.concatenate([tgt_feat, tgt_pot[None, :], log_tgt[None, :]], axis=0)
-    whole = lax.all_gather(packed, "cols", axis=1, tiled=True)
+    whole = turned_line(packed, "cols", 1)
     feats = whole[:D]
     ynorm = jnp.sum(feats * feats, axis=0)
     tblocks = whole.shape[1] // BLK

time: 665 us -> 653 us (0.982)
  between operations: 14.2 us -> 0.95 us
  waiting for transfers between devices: 46.1 us -> 56.6 us
  blocking collectives: 146 us -> 138 us
    ppermute x0 -> x7, waiting for transfers between devices: none -> 56.6 us  [turned_line(): terms = [lax.ppermute(terms[0], axis, right), *terms]]
    all_gather x1 -> x0, waiting for transfers between devices: 46.1 us -> none  [on_device(): whole = lax.all_gather(packed, 'cols', axis=1, tiled=True)]
    all_gather x2, blocking collectives: 146 us -> 138 us  [joined(): everything = jax.tree.map(lambda part: lax.all_gather(part, axis), array)]
  transfers between devices with their start and end apart: 1 -> 7, of which waited for: 1 -> 7; matrix products, arithmetic and copies ran while one was open for 0% -> 0% of each run, Pallas kernels for 0% -> 0%
where the time goes in v1:
time: 653 us; the launch traced here: 645 us
  matrix products  216 us (33%)
  blocking collectives  138 us (21%)
  other arithmetic  121 us (19%)
  loops' own time  57.5 us (9%)
  waiting for transfers between devices  56.6 us (9%)
  local copies, waits for them, and re-layouts  51.6 us (8%)
    dot_general x76, matrix products, take_group(): jnp.einsum('dr,gdc->rgc', xs, group[:, :D, :], precision=lax.Precision.HI...  198 us
    all_gather x2, blocking collectives, joined(): everything = jax.tree.map(lambda part: lax.all_gather(part, axis), array)  138 us
    ppermute x7, waiting for transfers between devices, turned_line(): terms = [lax.ppermute(terms[0], axis, right), *terms]  56.6 us
    another operation x1, loops' own time, on_device(): lax.scan(row_step, init, jnp.arange(pairs.shape[0], dtype=jnp.int32))  51.6 us
    lt x76, other arithmetic, take_group(): mask = jnp.repeat(step * GROUP + within < count, BLK)  48.4 us
    reduce_sum x38, other arithmetic, row_pass(): jnp.sum(jnp.exp(scores - top[:, None]), axis=1)  13.7 us
    select_n x32, other arithmetic, row_step(): slabs = jnp.take(blocks, row_ids, axis=0)  13.3 us
  transfers between devices with their start and end apart: 7, of which 7 were waited for; matrix products, arithmetic and copies ran while one was open for 0% of the time, Pallas kernels for 0%

profile of v1, /device:TPU:0, one launch (start us, length us, event | category | flops | bytes accessed | tf_op | source)
XLA Modules:
  0.0 644.9 jit_solution(18219105996446906004)
XLA Ops:
  11.9 8.1 %collective-permute-done.1 = f32[34,1024]{1,0:T(8,128)S(1)} collective-permute-done((f32[34,1024]{1,0:T(8,128)S(1)}, f32[34,1024]{1,0:T(8,128)S(1)}, u32[]{:S(2)}, u32[]{:S(2)}) %collective-permute-start.1) | collective-permute-done | bytes 139296 | tf_op jit(solution)/shard_map/ppermute | solution.py:18
  20.0 8.0 %collective-permute-done.2 = f32[34,1024]{1,0:T(8,128)S(1)} collective-permute-done((f32[34,1024]{1,0:T(8,128)S(1)}, f32[34,1024]{1,0:T(8,128)S(1)}, u32[]{:S(2)}, u32[]{:S(2)}) %collective-permute-start.2) | collective-permute-done | bytes 139296 | tf_op jit(solution)/shard_map/ppermute | solution.py:18
  28.0 8.0 %collective-permute-done.3 = f32[34,1024]{1,0:T(8,128)S(1)} collective-permute-done((f32[34,1024]{1,0:T(8,128)S(1)}, f32[34,1024]{1,0:T(8,128)S(1)}, u32[]{:S(2)}, u32[]{:S(2)}) %collective-permute-start.3) | collective-permute-done | bytes 139296 | tf_op jit(solution)/shard_map/ppermute | solution.py:18
  36.0 8.0 %collective-permute-done.4 = f32[34,1024]{1,0:T(8,128)S(1)} collective-permute-done((f32[34,1024]{1,0:T(8,128)S(1)}, f32[34,1024]{1,0:T(8,128)S(1)}, u32[]{:S(2)}, u32[]{:S(2)}) %collective-permute-start.4) | collective-permute-done | bytes 139296 | tf_op jit(solution)/shard_map/ppermute | solution.py:18
  44.1 9.2 %collective-permute-done.5 = f32[34,1024]{1,0:T(8,128)S(1)} collective-permute-done((f32[34,1024]{1,0:T(8,128)S(1)}, f32[34,1024]{1,0:T(8,128)S(1)}, u32[]{:S(2)}, u32[]{:S(2)}) %collective-permute-start.5) | collective-permute-done | bytes 139296 | tf_op jit(solution)/shard_map/ppermute | solution.py:18
  53.3 8.0 %collective-permute-done.6 = f32[34,1024]{1,0:T(8,128)S(1)} collective-permute-done((f32[34,1024]{1,0:T(8,128)S(1)}, f32[34,1024]{1,0:T(8,128)S(1)}, u32[]{:S(2)}, u32[]{:S(2)}) %collective-permute-start.6) | collective-permute-done | bytes 139296 | tf_op jit(solution)/shard_map/ppermute | solution.py:18
  63.3 439.5 %while.113 = (s32[]{:T(128)}, f32[32,256]{1,0:T(8,128)S(1)}, f32[32,256]{1,0:T(8,128)S(1)}, f32[16,256]{1,0:T(8,128)S(1)}, s32[16]{0:T(128)S(1)}, /*index=5*/s32...) while((s32[]{:T(128)}, f32[32,256]{1,0:T(8,128)S(1)}, ...), condition=%wide.region_12.13_spmd.clone.clone, body=%wide.region_1.12_spmd.clone.clone.sunk | while | flops 415103776 | bytes 13110493 | solution.py:127
  70.7 12.0 %while.114 = (s32[]{:T(128)}, f32[256]{0:T(256)S(1)}, f32[256]{0:T(256)S(1)}, s32[]{:T(128)}, s32[8]{0:T(128)S(1)}, /*index=5*/s32[]{:T(128)}, f32[24,35,256]{2,...) while((s32[]{:T(128)}, f32[256]{0:T(256)S(1)}, ...), condition=%wide.region_6.6_spmd, body=%wide.region_3.5_spmd.sunk | while | flops 206570016 | bytes 4627243 | solution.py:89
  83.4 12.3 %while.115 = (s32[]{:T(128)}, f32[32,256]{1,0:T(8,128)S(1)}, f32[32,256]{1,0:T(8,128)S(1)}, s32[]{:T(128)}, s32[24]{0:T(128)S(1)}, /*index=5*/s32[32]{0:T(128)S(...) while((s32[]{:T(128)}, f32[32,256]{1,0:T(8,128)S(1)}, ...), condition=%wide.region_11.11_spmd, body=%wide.region_7.10_spmd.sunk | while | flops 208300816 | bytes 4961095 | solution.py:123
  119.5 12.0 %while.114 = (s32[]{:T(128)}, f32[256]{0:T(256)S(1)}, f32[256]{0:T(256)S(1)}, s32[]{:T(128)}, s32[8]{0:T(128)S(1)}, /*index=5*/s32[]{:T(128)}, f32[24,35,256]{2,...) while((s32[]{:T(128)}, f32[256]{0:T(256)S(1)}, ...), condition=%wide.region_6.6_spmd, body=%wide.region_3.5_spmd.sunk | while | flops 206570016 | bytes 4627243 | solution.py:89
  132.3 12.3 %while.115 = (s32[]{:T(128)}, f32[32,256]{1,0:T(8,128)S(1)}, f32[32,256]{1,0:T(8,128)S(1)}, s32[]{:T(128)}, s32[24]{0:T(128)S(1)}, /*index=5*/s32[32]{0:T(128)S(...) while((s32[]{:T(128)}, f32[32,256]{1,0:T(8,128)S(1)}, ...), condition=%wide.region_11.11_spmd, body=%wide.region_7.10_spmd.sunk | while | flops 208300816 | bytes 4961095 | solution.py:123
  160.9 8.2 %while.115 = (s32[]{:T(128)}, f32[32,256]{1,0:T(8,128)S(1)}, f32[32,256]{1,0:T(8,128)S(1)}, s32[]{:T(128)}, s32[24]{0:T(128)S(1)}, /*index=5*/s32[32]{0:T(128)S(...) while((s32[]{:T(128)}, f32[32,256]{1,0:T(8,128)S(1)}, ...), condition=%wide.region_11.11_spmd, body=%wide.region_7.10_spmd.sunk | while | flops 208300816 | bytes 4961095 | solution.py:123
  176.5 12.0 %while.114 = (s32[]{:T(128)}, f32[256]{0:T(256)S(1)}, f32[256]{0:T(256)S(1)}, s32[]{:T(128)}, s32[8]{0:T(128)S(1)}, /*index=5*/s32[]{:T(128)}, f32[24,35,256]{2,...) while((s32[]{:T(128)}, f32[256]{0:T(256)S(1)}, ...), condition=%wide.region_6.6_spmd, body=%wide.region_3.5_spmd.sunk | while | flops 206570016 | bytes 4627243 | solution.py:89
  189.3 12.3 %while.115 = (s32[]{:T(128)}, f32[32,256]{1,0:T(8,128)S(1)}, f32[32,256]{1,0:T(8,128)S(1)}, s32[]{:T(128)}, s32[24]{0:T(128)S(1)}, /*index=5*/s32[32]{0:T(128)S(...) while((s32[]{:T(128)}, f32[32,256]{1,0:T(8,128)S(1)}, ...), condition=%wide.region_11.11_spmd, body=%wide.region_7.10_spmd.sunk | while | flops 208300816 | bytes 4961095 | solution.py:123
  209.0 12.0 %while.114 = (s32[]{:T(128)}, f32[256]{0:T(256)S(1)}, f32[256]{0:T(256)S(1)}, s32[]{:T(128)}, s32[8]{0:T(128)S(1)}, /*index=5*/s32[]{:T(128)}, f32[24,35,256]{2,...) while((s32[]{:T(128)}, f32[256]{0:T(256)S(1)}, ...), condition=%wide.region_6.6_spmd, body=%wide.region_3.5_spmd.sunk | while | flops 206570016 | bytes 4627243 | solution.py:89
  221.8 12.3 %while.115 = (s32[]{:T(128)}, f32[32,256]{1,0:T(8,128)S(1)}, f32[32,256]{1,0:T(8,128)S(1)}, s32[]{:T(128)}, s32[24]{0:T(128)S(1)}, /*index=5*/s32[32]{0:T(128)S(...) while((s32[]{:T(128)}, f32[32,256]{1,0:T(8,128)S(1)}, ...), condition=%wide.region_11.11_spmd, body=%wide.region_7.10_spmd.sunk | while | flops 208300816 | bytes 4961095 | solution.py:123
  250.4 8.2 %while.115 = (s32[]{:T(128)}, f32[32,256]{1,0:T(8,128)S(1)}, f32[32,256]{1,0:T(8,128)S(1)}, s32[]{:T(128)}, s32[24]{0:T(128)S(1)}, /*index=5*/s32[32]{0:T(128)S(...) while((s32[]{:T(128)}, f32[32,256]{1,0:T(8,128)S(1)}, ...), condition=%wide.region_11.11_spmd, body=%wide.region_7.10_spmd.sunk | while | flops 208300816 | bytes 4961095 | solution.py:123
  266.0 12.0 %while.114 = (s32[]{:T(128)}, f32[256]{0:T(256)S(1)}, f32[256]{0:T(256)S(1)}, s32[]{:T(128)}, s32[8]{0:T(128)S(1)}, /*index=5*/s32[]{:T(128)}, f32[24,35,256]{2,...) while((s32[]{:T(128)}, f32[256]{0:T(256)S(1)}, ...), condition=%wide.region_6.6_spmd, body=%wide.region_3.5_spmd.sunk | while | flops 206570016 | bytes 4627243 | solution.py:89
  278.8 12.3 %while.115 = (s32[]{:T(128)}, f32[32,256]{1,0:T(8,128)S(1)}, f32[32,256]{1,0:T(8,128)S(1)}, s32[]{:T(128)}, s32[24]{0:T(128)S(1)}, /*index=5*/s32[32]{0:T(128)S(...) while((s32[]{:T(128)}, f32[32,256]{1,0:T(8,128)S(1)}, ...), condition=%wide.region_11.11_spmd, body=%wide.region_7.10_spmd.sunk | while | flops 208300816 | bytes 4961095 | solution.py:123
  307.3 8.2 %while.115 = (s32[]{:T(128)}, f32[32,256]{1,0:T(8,128)S(1)}, f32[32,256]{1,0:T(8,128)S(1)}, s32[]{:T(128)}, s32[24]{0:T(128)S(1)}, /*index=5*/s32[32]{0:T(128)S(...) while((s32[]{:T(128)}, f32[32,256]{1,0:T(8,128)S(1)}, ...), condition=%wide.region_11.11_spmd, body=%wide.region_7.10_spmd.sunk | while | flops 208300816 | bytes 4961095 | solution.py:123
  331.8 8.2 %while.115 = (s32[]{:T(128)}, f32[32,256]{1,0:T(8,128)S(1)}, f32[32,256]{1,0:T(8,128)S(1)}, s32[]{:T(128)}, s32[24]{0:T(128)S(1)}, /*index=5*/s32[32]{0:T(128)S(...) while((s32[]{:T(128)}, f32[32,256]{1,0:T(8,128)S(1)}, ...), condition=%wide.region_11.11_spmd, body=%wide.region_7.10_spmd.sunk | while | flops 208300816 | bytes 4961095 | solution.py:123
  356.2 8.2 %while.115 = (s32[]{:T(128)}, f32[32,256]{1,0:T(8,128)S(1)}, f32[32,256]{1,0:T(8,128)S(1)}, s32[]{:T(128)}, s32[24]{0:T(128)S(1)}, /*index=5*/s32[32]{0:T(128)S(...) while((s32[]{:T(128)}, f32[32,256]{1,0:T(8,128)S(1)}, ...), condition=%wide.region_11.11_spmd, body=%wide.region_7.10_spmd.sunk | while | flops 208300816 | bytes 4961095 | solution.py:123
  380.6 8.2 %while.115 = (s32[]{:T(128)}, f32[32,256]{1,0:T(8,128)S(1)}, f32[32,256]{1,0:T(8,128)S(1)}, s32[]{:T(128)}, s32[24]{0:T(128)S(1)}, /*index=5*/s32[32]{0:T(128)S(...) while((s32[]{:T(128)}, f32[32,256]{1,0:T(8,128)S(1)}, ...), condition=%wide.region_11.11_spmd, body=%wide.region_7.10_spmd.sunk | while | flops 208300816 | bytes 4961095 | solution.py:123
  405.1 8.2 %while.115 = (s32[]{:T(128)}, f32[32,256]{1,0:T(8,128)S(1)}, f32[32,256]{1,0:T(8,128)S(1)}, s32[]{:T(128)}, s32[24]{0:T(128)S(1)}, /*index=5*/s32[32]{0:T(128)S(...) while((s32[]{:T(128)}, f32[32,256]{1,0:T(8,128)S(1)}, ...), condition=%wide.region_11.11_spmd, body=%wide.region_7.10_spmd.sunk | while | flops 208300816 | bytes 4961095 | solution.py:123
  420.7 12.0 %while.114 = (s32[]{:T(128)}, f32[256]{0:T(256)S(1)}, f32[256]{0:T(256)S(1)}, s32[]{:T(128)}, s32[8]{0:T(128)S(1)}, /*index=5*/s32[]{:T(128)}, f32[24,35,256]{2,...) while((s32[]{:T(128)}, f32[256]{0:T(256)S(1)}, ...), condition=%wide.region_6.6_spmd, body=%wide.region_3.5_spmd.sunk | while | flops 206570016 | bytes 4627243 | solution.py:89
  433.5 12.3 %while.115 = (s32[]{:T(128)}, f32[32,256]{1,0:T(8,128)S(1)}, f32[32,256]{1,0:T(8,128)S(1)}, s32[]{:T(128)}, s32[24]{0:T(128)S(1)}, /*index=5*/s32[32]{0:T(128)S(...) while((s32[]{:T(128)}, f32[32,256]{1,0:T(8,128)S(1)}, ...), condition=%wide.region_11.11_spmd, body=%wide.region_7.10_spmd.sunk | while | flops 208300816 | bytes 4961095 | solution.py:123
  453.2 12.0 %while.114 = (s32[]{:T(128)}, f32[256]{0:T(256)S(1)}, f32[256]{0:T(256)S(1)}, s32[]{:T(128)}, s32[8]{0:T(128)S(1)}, /*index=5*/s32[]{:T(128)}, f32[24,35,256]{2,...) while((s32[]{:T(128)}, f32[256]{0:T(256)S(1)}, ...), condition=%wide.region_6.6_spmd, body=%wide.region_3.5_spmd.sunk | while | flops 206570016 | bytes 4627243 | solution.py:89
  466.0 12.3 %while.115 = (s32[]{:T(128)}, f32[32,256]{1,0:T(8,128)S(1)}, f32[32,256]{1,0:T(8,128)S(1)}, s32[]{:T(128)}, s32[24]{0:T(128)S(1)}, /*index=5*/s32[32]{0:T(128)S(...) while((s32[]{:T(128)}, f32[32,256]{1,0:T(8,128)S(1)}, ...), condition=%wide.region_11.11_spmd, body=%wide.region_7.10_spmd.sunk | while | flops 208300816 | bytes 4961095 | solution.py:123
  485.8 8.0 %while.114 = (s32[]{:T(128)}, f32[256]{0:T(256)S(1)}, f32[256]{0:T(256)S(1)}, s32[]{:T(128)}, s32[8]{0:T(128)S(1)}, /*index=5*/s32[]{:T(128)}, f32[24,35,256]{2,...) while((s32[]{:T(128)}, f32[256]{0:T(256)S(1)}, ...), condition=%wide.region_6.6_spmd, body=%wide.region_3.5_spmd.sunk | while | flops 206570016 | bytes 4627243 | solution.py:89
  494.6 8.2 %while.115 = (s32[]{:T(128)}, f32[32,256]{1,0:T(8,128)S(1)}, f32[32,256]{1,0:T(8,128)S(1)}, s32[]{:T(128)}, s32[24]{0:T(128)S(1)}, /*index=5*/s32[32]{0:T(128)S(...) while((s32[]{:T(128)}, f32[32,256]{1,0:T(8,128)S(1)}, ...), condition=%wide.region_11.11_spmd, body=%wide.region_7.10_spmd.sunk | while | flops 208300816 | bytes 4961095 | solution.py:123
  502.9 104.4 %all-gather.1 = f32[16,1,8192]{2,1,0:T(1,128)S(1)} all-gather(f32[1,1,8192]{2,1,0:T(1,128)S(1)} %reshape.237), channel_id=1, replica_groups=mesh['parts'=2,'rows'=2,'cols'=8] {'rows','cols'}, dimensions={0}, use_global_device_ids=true | all-gather | bytes 557056 | tf_op jit(solution)/shard_map/all_gather | solution.py:25
  607.6 33.9 %all-gather = f32[16,1,8192]{2,1,0:T(1,128)S(1)} all-gather(f32[1,1,8192]{2,1,0:T(1,128)S(1)} %reshape.235), channel_id=1, replica_groups=mesh['parts'=2,'rows'=2,'cols'=8] {'rows','cols'}, dimensions={0}, use_global_device_ids=true | all-gather | bytes 557056 | tf_op jit(solution)/shard_map/all_gather | solution.py:25
  (1130 shorter events, 464.6 us)
Async XLA Ops:
  0.6 60.8 %copy-start.2 = (f32[1024]{0:T(1024)S(1)}, f32[1024]{0:T(1024)}, u32[]{:S(2)}) copy-start(f32[1024]{0:T(1024)} %param.17) | copy-start | bytes 12292
  0.6 60.8 %copy-start.1 = (f32[1024]{0:T(1024)S(1)}, f32[1024]{0:T(1024)}, u32[]{:S(2)}) copy-start(f32[1024]{0:T(1024)} %param.19) | copy-start | bytes 12292
  0.7 60.8 %copy-start = (f32[32,1024]{1,0:T(8,128)S(1)}, f32[32,1024]{1,0:T(8,128)}, u32[]{:S(2)}) copy-start(f32[32,1024]{1,0:T(8,128)} %param.16) | copy-start | bytes 393220
  1.7 10.3 %collective-permute-start = (f32[34,1024]{1,0:T(8,128)S(1)}, f32[34,1024]{1,0:T(8,128)S(1)}, u32[]{:S(2)}, u32[]{:S(2)}) collective-permute-start(f32[34,1024]{1,0:T(8,128)S(1)} %pad_maximum_fusion), channel_id=1, source_target_pairs={{0,1},{1,2},{2,3},{3,4},{4,5},{5,6},{6,7},{7,0},{8,9},{9,10},{10,1... | collective-permute-start | bytes 417800 | tf_op jit(solution)/shard_map/ppermute | solution.py:18
  11.9 8.1 %collective-permute-start.1 = (f32[34,1024]{1,0:T(8,128)S(1)}, f32[34,1024]{1,0:T(8,128)S(1)}, u32[]{:S(2)}, u32[]{:S(2)}) collective-permute-start(f32[34,1024]{1,0:T(8,128)S(1)} %collective-permute-done), channel_id=1, source_target_pairs={{0,1},{1,2},{2,3},{3,4},{4,5},{5,6},{6,7},{7,0},{8,9},{9,10},{10,1... | collective-permute-start | bytes 417800 | tf_op jit(solution)/shard_map/ppermute | solution.py:18
  20.0 8.0 %collective-permute-start.2 = (f32[34,1024]{1,0:T(8,128)S(1)}, f32[34,1024]{1,0:T(8,128)S(1)}, u32[]{:S(2)}, u32[]{:S(2)}) collective-permute-start(f32[34,1024]{1,0:T(8,128)S(1)} %collective-permute-done.1), channel_id=1, source_target_pairs={{0,1},{1,2},{2,3},{3,4},{4,5},{5,6},{6,7},{7,0},{8,9},{9,10},{10,1... | collective-permute-start | bytes 417800 | tf_op jit(solution)/shard_map/ppermute | solution.py:18
  28.0 8.0 %collective-permute-start.3 = (f32[34,1024]{1,0:T(8,128)S(1)}, f32[34,1024]{1,0:T(8,128)S(1)}, u32[]{:S(2)}, u32[]{:S(2)}) collective-permute-start(f32[34,1024]{1,0:T(8,128)S(1)} %collective-permute-done.2), channel_id=1, source_target_pairs={{0,1},{1,2},{2,3},{3,4},{4,5},{5,6},{6,7},{7,0},{8,9},{9,10},{10,1... | collective-permute-start | bytes 417800 | tf_op jit(solution)/shard_map/ppermute | solution.py:18
  36.0 8.0 %collective-permute-start.4 = (f32[34,1024]{1,0:T(8,128)S(1)}, f32[34,1024]{1,0:T(8,128)S(1)}, u32[]{:S(2)}, u32[]{:S(2)}) collective-permute-start(f32[34,1024]{1,0:T(8,128)S(1)} %collective-permute-done.3), channel_id=1, source_target_pairs={{0,1},{1,2},{2,3},{3,4},{4,5},{5,6},{6,7},{7,0},{8,9},{9,10},{10,1... | collective-permute-start | bytes 417800 | tf_op jit(solution)/shard_map/ppermute | solution.py:18
  44.1 9.2 %collective-permute-start.5 = (f32[34,1024]{1,0:T(8,128)S(1)}, f32[34,1024]{1,0:T(8,128)S(1)}, u32[]{:S(2)}, u32[]{:S(2)}) collective-permute-start(f32[34,1024]{1,0:T(8,128)S(1)} %collective-permute-done.4), channel_id=1, source_target_pairs={{0,1},{1,2},{2,3},{3,4},{4,5},{5,6},{6,7},{7,0},{8,9},{9,10},{10,1... | collective-permute-start | bytes 417800 | tf_op jit(solution)/shard_map/ppermute | solution.py:18
  53.3 8.0 %collective-permute-start.6 = (f32[34,1024]{1,0:T(8,128)S(1)}, f32[34,1024]{1,0:T(8,128)S(1)}, u32[]{:S(2)}, u32[]{:S(2)}) collective-permute-start(f32[34,1024]{1,0:T(8,128)S(1)} %collective-permute-done.5), channel_id=1, source_target_pairs={{0,1},{1,2},{2,3},{3,4},{4,5},{5,6},{6,7},{7,0},{8,9},{9,10},{10,1... | collective-permute-start | bytes 417800 | tf_op jit(solution)/shard_map/ppermute | solution.py:18
  62.5 0.8 copy-start.3
